TPU v7x, 512 devices: a whole 4x4x16 slice. The times are simulated.
512 devices in a mesh: row: 32 (over z, core), band: 16 (over y, x).
Axes of the slice: x: 4, y: 4, z: 16, core: 2. Of those that a mesh axis runs over, the one named last changes fastest.
Arguments:
- band_blocks: bfloat16 [1024, 16, 128, 128], P('row', 'band'), may hold values from 0 to 0.006591797, as said below
- distant_block_slots: bfloat16 [32, 16, 32, 2, 128, 128], P('row', 'band'), may hold values from 0 to 0.00033203125, as said below
- far_rows: int32 [32, 16, 32, 2], P('row', 'band'), may hold values from 0 to 31
- far_columns: int32 [32, 16, 32, 2], P('row', 'band'), may hold values from 0 to 31
- far_counts: int32 [32, 16, 32], P('row', 'band'), may hold values from 0 to 2, as said below
Outputs:
- scaling: float32 [1024, 128], P('row')
- residual: float32 [1024, 128], P('row')
Inputs may be any that keep to these rules, and one draw needn't show every extreme that they name: `band_blocks`: positive entries; offset-0 blocks symmetric. `distant_block_slots`: positive entries. `far_counts`: some target range receives 2 live slots from every device.
All inputs are finite; a program needn't handle non-finite values.
Results may differ from a plain program's by a relative error of at most 0.0116.
The roundings to bfloat16 on the way count: a program that leaves them out, or rounds other values in their place, can miss the bound.
Values may be sent and summed in bfloat16 or wider, within the bound.
No kernel may reach another device: no remote copies, remote signals or barrier semaphores. Data moves between devices by JAX's collectives and lax.ppermute only.
A program may use at most 64 MiB of HBM per device.

v0:
```python
import jax
import jax.numpy as jnp
from jax import lax
from jax.sharding import PartitionSpec as P

OUTER = 2
INNER = 2


def shifted(value, axis, steps):
    count = lax.axis_size(axis)
    leading, last = (max(0, -steps), min(count, count - steps))
    return lax.ppermute(value, axis, [(source, source + steps) for source in range(leading, last)])


def on_device(band_blocks, distant_block_slots, far_rows, far_columns, far_counts):
    rows_dev = band_blocks.shape[0]
    block_size = band_blocks.shape[2]
    band_count = lax.axis_size("band")
    row_count = lax.axis_size("row")
    offset = lax.axis_index("band")
    row_index = lax.axis_index("row")
    blocks = band_blocks[:, 0]
    distant_local_part = distant_block_slots[0, 0]
    local_row_values = far_rows[0, 0]
    columns_local = far_columns[0, 0]
    counts = far_counts[0, 0]
    slots = local_row_values.shape[1]
    live_mask = (jnp.arange(slots)[None, :] < counts[:, None]).astype(jnp.float32)[..., None]
    block_ids = row_index * rows_dev + jnp.arange(rows_dev)
    valid_mask = (block_ids + offset < row_count * rows_dev).astype(jnp.float32)[:, None]
    upper_mask = (offset > 0).astype(jnp.float32)
    wanted = lax.all_to_all(columns_local, "row", split_axis=0, concat_axis=0, tiled=True)
    targets = jnp.arange(rows_dev)[None, :]
    selection_output = (wanted.reshape(-1)[:, None] == targets).astype(jnp.float32)
    pick_in = (local_row_values.reshape(-1)[:, None] == targets).astype(jnp.float32)

    def multiply(vector):
        narrow_band_part = vector.astype(jnp.bfloat16)
        ahead_rows = shifted(narrow_band_part[:band_count], "row", -1)
        extended = jnp.concatenate([narrow_band_part, ahead_rows], 0)
        columns = lax.dynamic_slice_in_dim(extended, offset, rows_dev, 0)
        forward = (
            jnp.einsum("kij,kj->ki", blocks, columns, preferred_element_type=jnp.float32)
            * valid_mask
        )
        backward = jnp.einsum(
            "kij,ki->kj", blocks, narrow_band_part, preferred_element_type=jnp.float32
        ) * (valid_mask * upper_mask)
        spread = lax.dynamic_update_slice_in_dim(
            jnp.zeros((rows_dev + band_count, block_size), jnp.float32), backward, offset, 0
        )
        outgoing = narrow_band_part[wanted]
        gathered_values = lax.all_to_all(outgoing, "row", split_axis=0, concat_axis=0, tiled=True)
        far_forward = (
            jnp.einsum(
                "oqht,oqt->oqh",
                distant_local_part,
                gathered_values,
                preferred_element_type=jnp.float32,
            )
            * live_mask
        )
        far_backward = (
            jnp.einsum(
                "nquo,nqu->nqo",
                distant_local_part,
                narrow_band_part[local_row_values],
                preferred_element_type=jnp.float32,
            )
            * live_mask
        )
        returned = lax.all_to_all(far_backward, "row", split_axis=0, concat_axis=0, tiled=True)
        summed = forward + spread[:rows_dev]
        summed = summed + jnp.dot(
            pick_in.T, far_forward.reshape(-1, block_size), precision=lax.Precision.HIGHEST
        )
        summed = summed + jnp.dot(
            selection_output.T, returned.reshape(-1, block_size), precision=lax.Precision.HIGHEST
        )
        carried = shifted(spread[rows_dev:], "row", 1)
        summed = jnp.concatenate([summed[:band_count] + carried, summed[band_count:]], 0)
        return lax.psum(summed, "band")

    row_sums = multiply(jnp.ones((rows_dev, block_size), jnp.float32))
    scaling = 1.0 / jnp.sqrt(row_sums)
    residual = jnp.zeros_like(scaling)
    for outer_step in range(OUTER):
        balance = scaling * multiply(scaling)
        residual = 1.0 - balance
        scaled = residual / balance
        direction = scaled
        current_residual_product = lax.psum(jnp.sum(residual * scaled), "row")
        growth = jnp.ones_like(scaling)
        for inner_step in range(INNER):
            curved = scaling * multiply(scaling * direction) + balance * direction
            curvature = lax.psum(jnp.sum(direction * curved), "row")
            step_size = current_residual_product / curvature
            growth = growth + step_size * direction
            residual = residual - step_size * curved
            if inner_step + 1 < INNER:
                scaled = residual / balance
                rho_next = lax.psum(jnp.sum(residual * scaled), "row")
                direction = scaled + rho_next / current_residual_product * direction
                current_residual_product = rho_next
        scaling = scaling * growth
    return (scaling, residual)


def solution(mesh):
    return jax.shard_map(
        on_device,
        mesh=mesh,
        in_specs=(
            P("row", "band", None, None),
            P("row", "band", None, None, None, None),
            P("row", "band", None, None),
            P("row", "band", None, None),
            P("row", "band", None),
        ),
        out_specs=(P("row", None), P("row", None)),
        check_vma=False,
    )
```

profile of v0, /device:TPU:1, one launch (start us, length us, event | category | flops | bytes accessed | tf_op | source)
XLA Modules:
  0.0 1086.6 jit_solution(9231055719620302037)
XLA Ops:
  11.1 10.0 all-to-all-start
  59.5 12.0 %all-to-all-done.2 = f32[32,2,128]{2,1,0:T(2,128)S(1)} async-done(((f32[32,2,128]{2,1,0:T(2,128)}), f32[32,2,128]{2,1,0:T(2,128)S(1)}, u32[]{:S(2)}, u32[]{:S(2)}) %all-to-all-start.2) | async-done | bytes 32800 | tf_op jit(solution)/shard_map/all_to_all | solution.py:73
  71.8 60.6 %psum.105 = f32[32,128]{1,0:T(8,128)S(1)} all-reduce(f32[32,128]{1,0:T(8,128)S(1)} %pad_maximum_fusion), channel_id=1, replica_groups=mesh['row'=32,'band'=16] {'band'}, use_global_device_ids=true, to_apply=%region_0.0 | all-reduce | flops 4096 | bytes 32768 | tf_op jit(solution)/shard_map/psum | solution.py:83
  134.3 16.9 %collective-permute-start.2 = (bf16[16,128]{1,0:T(8,128)(2,1)S(1)}, bf16[16,128]{1,0:T(8,128)(2,1)S(1)}, u32[]{:S(2)}, u32[]{:S(2)}) collective-permute-start(bf16[16,128]{1,0:T(8,128)(2,1)S(1)} %slice.172), channel_id=1, source_target_pairs={{16,0},{32,16},{48,32},{64,48},{80,64},{96,80},{112,96},{128,112},... | collective-permute-start | bytes 12296 | tf_op jit(solution)/shard_map/ppermute | solution.py:13
  172.8 11.8 %all-to-all-done.4 = f32[32,2,128]{2,1,0:T(2,128)S(1)} async-done(((f32[32,2,128]{2,1,0:T(2,128)}), f32[32,2,128]{2,1,0:T(2,128)S(1)}, u32[]{:S(2)}, u32[]{:S(2)}) %all-to-all-start.4) | async-done | bytes 32800 | tf_op jit(solution)/shard_map/all_to_all | solution.py:73
  184.9 55.9 %psum.106 = f32[32,128]{1,0:T(8,128)S(1)} all-reduce(f32[32,128]{1,0:T(8,128)S(1)} %pad_maximum_fusion.1), channel_id=1, replica_groups=mesh['row'=32,'band'=16] {'band'}, use_global_device_ids=true, to_apply=%region_1.0 | all-reduce | flops 4096 | bytes 32768 | tf_op jit(solution)/shard_map/psum | solution.py:83
  242.7 16.7 %collective-permute-start.4 = (bf16[16,128]{1,0:T(8,128)(2,1)S(1)}, bf16[16,128]{1,0:T(8,128)(2,1)S(1)}, u32[]{:S(2)}, u32[]{:S(2)}) collective-permute-start(bf16[16,128]{1,0:T(8,128)(2,1)S(1)} %slice.177), channel_id=1, source_target_pairs={{16,0},{32,16},{48,32},{64,48},{80,64},{96,80},{112,96},{128,112},... | collective-permute-start | bytes 12296 | tf_op jit(solution)/shard_map/ppermute | solution.py:13
  281.0 11.8 %all-to-all-done.6 = f32[32,2,128]{2,1,0:T(2,128)S(1)} async-done(((f32[32,2,128]{2,1,0:T(2,128)}), f32[32,2,128]{2,1,0:T(2,128)S(1)}, u32[]{:S(2)}, u32[]{:S(2)}) %all-to-all-start.6) | async-done | bytes 32800 | tf_op jit(solution)/shard_map/all_to_all | solution.py:73
  293.1 55.9 %psum.108 = f32[32,128]{1,0:T(8,128)S(1)} all-reduce(f32[32,128]{1,0:T(8,128)S(1)} %pad_maximum_fusion.2), channel_id=1, replica_groups=mesh['row'=32,'band'=16] {'band'}, use_global_device_ids=true, to_apply=%region_4.0 | all-reduce | flops 4096 | bytes 32768 | tf_op jit(solution)/shard_map/psum | solution.py:83
  349.6 60.6 %all-reduce.2 = (f32[]{:T(128)}, f32[]{:T(128)}) all-reduce(f32[]{:T(128)} %get-tuple-element.3, f32[]{:T(128)} %get-tuple-element.2), channel_id=1, replica_groups=mesh['row'=32,'band'=16] {'row'}, use_global_device_ids=true, to_apply=%region_3.0 | all-reduce | flops 2 | bytes 16 | tf_op jit(solution)/shard_map/psum | solution.py:93
  412.1 46.4 %psum.110 = f32[]{:T(128)} all-reduce(f32[]{:T(128)} %multiply_reduce_fusion.4), channel_id=1, replica_groups=mesh['row'=32,'band'=16] {'row'}, use_global_device_ids=true, to_apply=%region_8.0 | all-reduce | flops 1 | bytes 8 | tf_op jit(solution)/shard_map/psum | solution.py:103
  486.0 11.8 %all-to-all-done.8 = f32[32,2,128]{2,1,0:T(2,128)S(1)} async-done(((f32[32,2,128]{2,1,0:T(2,128)}), f32[32,2,128]{2,1,0:T(2,128)S(1)}, u32[]{:S(2)}, u32[]{:S(2)}) %all-to-all-start.8) | async-done | bytes 32800 | tf_op jit(solution)/shard_map/all_to_all | solution.py:73
  498.1 55.9 %psum.111 = f32[32,128]{1,0:T(8,128)S(1)} all-reduce(f32[32,128]{1,0:T(8,128)S(1)} %pad_maximum_fusion.3), channel_id=1, replica_groups=mesh['row'=32,'band'=16] {'band'}, use_global_device_ids=true, to_apply=%region_9.0 | all-reduce | flops 4096 | bytes 32768 | tf_op jit(solution)/shard_map/psum | solution.py:83
  554.6 60.6 %psum.112 = f32[]{:T(128)} all-reduce(f32[]{:T(128)} %multiply_reduce_fusion.3), channel_id=1, replica_groups=mesh['row'=32,'band'=16] {'row'}, use_global_device_ids=true, to_apply=%region_11.0 | all-reduce | flops 1 | bytes 8 | tf_op jit(solution)/shard_map/psum | solution.py:97
  642.5 11.8 %all-to-all-done.10 = f32[32,2,128]{2,1,0:T(2,128)S(1)} async-done(((f32[32,2,128]{2,1,0:T(2,128)}), f32[32,2,128]{2,1,0:T(2,128)S(1)}, u32[]{:S(2)}, u32[]{:S(2)}) %all-to-all-start.10) | async-done | bytes 32800 | tf_op jit(solution)/shard_map/all_to_all | solution.py:73
  654.6 55.9 %psum.113 = f32[32,128]{1,0:T(8,128)S(1)} all-reduce(f32[32,128]{1,0:T(8,128)S(1)} %pad_maximum_fusion.4), channel_id=1, replica_groups=mesh['row'=32,'band'=16] {'band'}, use_global_device_ids=true, to_apply=%region_12.0 | all-reduce | flops 4096 | bytes 32768 | tf_op jit(solution)/shard_map/psum | solution.py:83
  712.4 16.7 %collective-permute-start.10 = (bf16[16,128]{1,0:T(8,128)(2,1)S(1)}, bf16[16,128]{1,0:T(8,128)(2,1)S(1)}, u32[]{:S(2)}, u32[]{:S(2)}) collective-permute-start(bf16[16,128]{1,0:T(8,128)(2,1)S(1)} %slice.192), channel_id=1, source_target_pairs={{16,0},{32,16},{48,32},{64,48},{80,64},{96,80},{112,96},{128,112},... | collective-permute-start | bytes 12296 | tf_op jit(solution)/shard_map/ppermute | solution.py:13
  750.7 11.8 %all-to-all-done.12 = f32[32,2,128]{2,1,0:T(2,128)S(1)} async-done(((f32[32,2,128]{2,1,0:T(2,128)}), f32[32,2,128]{2,1,0:T(2,128)S(1)}, u32[]{:S(2)}, u32[]{:S(2)}) %all-to-all-start.12) | async-done | bytes 32800 | tf_op jit(solution)/shard_map/all_to_all | solution.py:73
  762.8 55.9 %psum.115 = f32[32,128]{1,0:T(8,128)S(1)} all-reduce(f32[32,128]{1,0:T(8,128)S(1)} %pad_maximum_fusion.5), channel_id=1, replica_groups=mesh['row'=32,'band'=16] {'band'}, use_global_device_ids=true, to_apply=%region_15.0 | all-reduce | flops 4096 | bytes 32768 | tf_op jit(solution)/shard_map/psum | solution.py:83
  819.3 60.6 %all-reduce.1 = (f32[]{:T(128)}, f32[]{:T(128)}) all-reduce(f32[]{:T(128)} %get-tuple-element.5, f32[]{:T(128)} %get-tuple-element.4), channel_id=1, replica_groups=mesh['row'=32,'band'=16] {'row'}, use_global_device_ids=true, to_apply=%region_14.0 | all-reduce | flops 2 | bytes 16 | tf_op jit(solution)/shard_map/psum | solution.py:93
  881.9 46.4 %psum.117 = f32[]{:T(128)} all-reduce(f32[]{:T(128)} %get-tuple-element.10), channel_id=1, replica_groups=mesh['row'=32,'band'=16] {'row'}, use_global_device_ids=true, to_apply=%region_19.0 | all-reduce | flops 1 | bytes 8 | tf_op jit(solution)/shard_map/psum | solution.py:103
  955.6 11.8 %all-to-all-done.14 = f32[32,2,128]{2,1,0:T(2,128)S(1)} async-done(((f32[32,2,128]{2,1,0:T(2,128)}), f32[32,2,128]{2,1,0:T(2,128)S(1)}, u32[]{:S(2)}, u32[]{:S(2)}) %all-to-all-start.14) | async-done | bytes 32800 | tf_op jit(solution)/shard_map/all_to_all | solution.py:73
  967.7 55.9 %psum.118 = f32[32,128]{1,0:T(8,128)S(1)} all-reduce(f32[32,128]{1,0:T(8,128)S(1)} %pad_maximum_fusion.6), channel_id=1, replica_groups=mesh['row'=32,'band'=16] {'band'}, use_global_device_ids=true, to_apply=%region_20.0 | all-reduce | flops 4096 | bytes 32768 | tf_op jit(solution)/shard_map/psum | solution.py:83
  1024.2 60.6 %psum.119 = f32[]{:T(128)} all-reduce(f32[]{:T(128)} %multiply_reduce_fusion), channel_id=1, replica_groups=mesh['row'=32,'band'=16] {'row'}, use_global_device_ids=true, to_apply=%region_22.0 | all-reduce | flops 1 | bytes 8 | tf_op jit(solution)/shard_map/psum | solution.py:97
  (202 shorter events, 203.3 us)
Async XLA Ops:
  0.7 43.3 %collective-permute-start = (bf16[16,128]{1,0:T(8,128)(2,1)S(1)}, bf16[16,128]{1,0:T(8,128)(2,1)S(1)}, u32[]{:S(2)}, u32[]{:S(2)}) collective-permute-start(bf16[16,128]{1,0:T(8,128)(2,1)S(1)} %slice.105), channel_id=1, source_target_pairs={{16,0},{32,16},{48,32},{64,48},{80,64},{96,80},{112,96},{128,112},... | collective-permute-start | bytes 12296 | tf_op jit(solution)/shard_map/ppermute | solution.py:13
  11.1 21.8 %all-to-all-start = ((s32[32,1,2]{2,1,0:T(1,128)}), s32[32,1,2]{2,1,0:T(1,128)S(1)}, u32[]{:S(2)}, u32[]{:S(2)}) async-start(s32[32,1,2]{2,1,0:T(1,128)} %copy.16), calls=%async_computation | async-start | bytes 32768 | tf_op jit(solution)/shard_map/all_to_all | solution.py:33
  23.0 48.8 %collective-permute-start.1 = (f32[16,128]{1,0:T(8,128)S(1)}, f32[16,128]{1,0:T(8,128)S(1)}, u32[]{:S(2)}, u32[]{:S(2)}) collective-permute-start(f32[16,128]{1,0:T(8,128)S(1)} %slice.170), channel_id=1, source_target_pairs={{0,16},{16,32},{32,48},{48,64},{64,80},{80,96},{96,112},{112,128},... | collective-permute-start | bytes 24584 | tf_op jit(solution)/shard_map/ppermute | solution.py:13
  35.0 17.9 %all-to-all-start.1 = ((bf16[32,2,128]{2,1,0:T(2,128)(2,1)}), bf16[32,2,128]{2,1,0:T(2,128)(2,1)S(1)}, u32[]{:S(2)}, u32[]{:S(2)}) async-start(bf16[32,2,128]{2,1,0:T(2,128)(2,1)} %bitcast.8), calls=%async_computation.1 | async-start | bytes 32768 | tf_op jit(solution)/shard_map/all_to_all | solution.py:54
  54.8 16.6 %all-to-all-start.2 = ((f32[32,2,128]{2,1,0:T(2,128)}), f32[32,2,128]{2,1,0:T(2,128)S(1)}, u32[]{:S(2)}, u32[]{:S(2)}) async-start(f32[32,2,128]{2,1,0:T(2,128)} %get-tuple-element.45), calls=%async_computation.2 | async-start | bytes 65536 | tf_op jit(solution)/shard_map/all_to_all | solution.py:73
  134.3 24.7 %collective-permute-start.2 = (bf16[16,128]{1,0:T(8,128)(2,1)S(1)}, bf16[16,128]{1,0:T(8,128)(2,1)S(1)}, u32[]{:S(2)}, u32[]{:S(2)}) collective-permute-start(bf16[16,128]{1,0:T(8,128)(2,1)S(1)} %slice.172), channel_id=1, source_target_pairs={{16,0},{32,16},{48,32},{64,48},{80,64},{96,80},{112,96},{128,112},... | collective-permute-start | bytes 12296 | tf_op jit(solution)/shard_map/ppermute | solution.py:13
  151.2 14.7 %all-to-all-start.3 = ((bf16[32,2,128]{2,1,0:T(2,128)(2,1)}), bf16[32,2,128]{2,1,0:T(2,128)(2,1)S(1)}, u32[]{:S(2)}, u32[]{:S(2)}) async-start(bf16[32,2,128]{2,1,0:T(2,128)(2,1)} %bitcast.27), calls=%async_computation.3 | async-start | bytes 32768 | tf_op jit(solution)/shard_map/all_to_all | solution.py:54
  156.2 28.7 %collective-permute-start.3 = (f32[16,128]{1,0:T(8,128)S(1)}, f32[16,128]{1,0:T(8,128)S(1)}, u32[]{:S(2)}, u32[]{:S(2)}) collective-permute-start(f32[16,128]{1,0:T(8,128)S(1)} %slice.175), channel_id=1, source_target_pairs={{0,16},{16,32},{32,48},{48,64},{64,80},{80,96},{96,112},{112,128},... | collective-permute-start | bytes 24584 | tf_op jit(solution)/shard_map/ppermute | solution.py:13
  167.8 16.8 %all-to-all-start.4 = ((f32[32,2,128]{2,1,0:T(2,128)}), f32[32,2,128]{2,1,0:T(2,128)S(1)}, u32[]{:S(2)}, u32[]{:S(2)}) async-start(f32[32,2,128]{2,1,0:T(2,128)} %get-tuple-element.41), calls=%async_computation.4 | async-start | bytes 65536 | tf_op jit(solution)/shard_map/all_to_all | solution.py:73
  242.7 24.5 %collective-permute-start.4 = (bf16[16,128]{1,0:T(8,128)(2,1)S(1)}, bf16[16,128]{1,0:T(8,128)(2,1)S(1)}, u32[]{:S(2)}, u32[]{:S(2)}) collective-permute-start(bf16[16,128]{1,0:T(8,128)(2,1)S(1)} %slice.177), channel_id=1, source_target_pairs={{16,0},{32,16},{48,32},{64,48},{80,64},{96,80},{112,96},{128,112},... | collective-permute-start | bytes 12296 | tf_op jit(solution)/shard_map/ppermute | solution.py:13
  259.4 14.7 %all-to-all-start.5 = ((bf16[32,2,128]{2,1,0:T(2,128)(2,1)}), bf16[32,2,128]{2,1,0:T(2,128)(2,1)S(1)}, u32[]{:S(2)}, u32[]{:S(2)}) async-start(bf16[32,2,128]{2,1,0:T(2,128)(2,1)} %bitcast.43), calls=%async_computation.5 | async-start | bytes 32768 | tf_op jit(solution)/shard_map/all_to_all | solution.py:54
  264.4 28.7 %collective-permute-start.5 = (f32[16,128]{1,0:T(8,128)S(1)}, f32[16,128]{1,0:T(8,128)S(1)}, u32[]{:S(2)}, u32[]{:S(2)}) collective-permute-start(f32[16,128]{1,0:T(8,128)S(1)} %slice.180), channel_id=1, source_target_pairs={{0,16},{16,32},{32,48},{48,64},{64,80},{80,96},{96,112},{112,128},... | collective-permute-start | bytes 24584 | tf_op jit(solution)/shard_map/ppermute | solution.py:13
  276.0 16.8 %all-to-all-start.6 = ((f32[32,2,128]{2,1,0:T(2,128)}), f32[32,2,128]{2,1,0:T(2,128)S(1)}, u32[]{:S(2)}, u32[]{:S(2)}) async-start(f32[32,2,128]{2,1,0:T(2,128)} %get-tuple-element.37), calls=%async_computation.6 | async-start | bytes 65536 | tf_op jit(solution)/shard_map/all_to_all | solution.py:73
  464.3 14.8 %all-to-all-start.7 = ((bf16[32,2,128]{2,1,0:T(2,128)(2,1)}), bf16[32,2,128]{2,1,0:T(2,128)(2,1)S(1)}, u32[]{:S(2)}, u32[]{:S(2)}) async-start(bf16[32,2,128]{2,1,0:T(2,128)(2,1)} %bitcast.59), calls=%async_computation.7 | async-start | bytes 32768 | tf_op jit(solution)/shard_map/all_to_all | solution.py:54
  469.4 28.7 %collective-permute-start.7 = (f32[16,128]{1,0:T(8,128)S(1)}, f32[16,128]{1,0:T(8,128)S(1)}, u32[]{:S(2)}, u32[]{:S(2)}) collective-permute-start(f32[16,128]{1,0:T(8,128)S(1)} %slice.185), channel_id=1, source_target_pairs={{0,16},{16,32},{32,48},{48,64},{64,80},{80,96},{96,112},{112,128},... | collective-permute-start | bytes 24584 | tf_op jit(solution)/shard_map/ppermute | solution.py:13
  481.0 16.8 %all-to-all-start.8 = ((f32[32,2,128]{2,1,0:T(2,128)}), f32[32,2,128]{2,1,0:T(2,128)S(1)}, u32[]{:S(2)}, u32[]{:S(2)}) async-start(f32[32,2,128]{2,1,0:T(2,128)} %get-tuple-element.33), calls=%async_computation.8 | async-start | bytes 65536 | tf_op jit(solution)/shard_map/all_to_all | solution.py:73
  625.9 28.7 %collective-permute-start.9 = (f32[16,128]{1,0:T(8,128)S(1)}, f32[16,128]{1,0:T(8,128)S(1)}, u32[]{:S(2)}, u32[]{:S(2)}) collective-permute-start(f32[16,128]{1,0:T(8,128)S(1)} %slice.190), channel_id=1, source_target_pairs={{0,16},{16,32},{32,48},{48,64},{64,80},{80,96},{96,112},{112,128},... | collective-permute-start | bytes 24584 | tf_op jit(solution)/shard_map/ppermute | solution.py:13
  637.5 16.8 %all-to-all-start.10 = ((f32[32,2,128]{2,1,0:T(2,128)}), f32[32,2,128]{2,1,0:T(2,128)S(1)}, u32[]{:S(2)}, u32[]{:S(2)}) async-start(f32[32,2,128]{2,1,0:T(2,128)} %get-tuple-element.29), calls=%async_computation.10 | async-start | bytes 65536 | tf_op jit(solution)/shard_map/all_to_all | solution.py:73
  712.4 24.5 %collective-permute-start.10 = (bf16[16,128]{1,0:T(8,128)(2,1)S(1)}, bf16[16,128]{1,0:T(8,128)(2,1)S(1)}, u32[]{:S(2)}, u32[]{:S(2)}) collective-permute-start(bf16[16,128]{1,0:T(8,128)(2,1)S(1)} %slice.192), channel_id=1, source_target_pairs={{16,0},{32,16},{48,32},{64,48},{80,64},{96,80},{112,96},{128,112},... | collective-permute-start | bytes 12296 | tf_op jit(solution)/shard_map/ppermute | solution.py:13
  729.1 14.7 %all-to-all-start.11 = ((bf16[32,2,128]{2,1,0:T(2,128)(2,1)}), bf16[32,2,128]{2,1,0:T(2,128)(2,1)S(1)}, u32[]{:S(2)}, u32[]{:S(2)}) async-start(bf16[32,2,128]{2,1,0:T(2,128)(2,1)} %bitcast.91), calls=%async_computation.11 | async-start | bytes 32768 | tf_op jit(solution)/shard_map/all_to_all | solution.py:54
  734.1 28.7 %collective-permute-start.11 = (f32[16,128]{1,0:T(8,128)S(1)}, f32[16,128]{1,0:T(8,128)S(1)}, u32[]{:S(2)}, u32[]{:S(2)}) collective-permute-start(f32[16,128]{1,0:T(8,128)S(1)} %slice.195), channel_id=1, source_target_pairs={{0,16},{16,32},{32,48},{48,64},{64,80},{80,96},{96,112},{112,128},... | collective-permute-start | bytes 24584 | tf_op jit(solution)/shard_map/ppermute | solution.py:13
  745.7 16.8 %all-to-all-start.12 = ((f32[32,2,128]{2,1,0:T(2,128)}), f32[32,2,128]{2,1,0:T(2,128)S(1)}, u32[]{:S(2)}, u32[]{:S(2)}) async-start(f32[32,2,128]{2,1,0:T(2,128)} %get-tuple-element.25), calls=%async_computation.12 | async-start | bytes 65536 | tf_op jit(solution)/shard_map/all_to_all | solution.py:73
  938.9 28.7 %collective-permute-start.13 = (f32[16,128]{1,0:T(8,128)S(1)}, f32[16,128]{1,0:T(8,128)S(1)}, u32[]{:S(2)}, u32[]{:S(2)}) collective-permute-start(f32[16,128]{1,0:T(8,128)S(1)} %slice.200), channel_id=1, source_target_pairs={{0,16},{16,32},{32,48},{48,64},{64,80},{80,96},{96,112},{112,128},... | collective-permute-start | bytes 24584 | tf_op jit(solution)/shard_map/ppermute | solution.py:13
  950.5 16.8 %all-to-all-start.14 = ((f32[32,2,128]{2,1,0:T(2,128)}), f32[32,2,128]{2,1,0:T(2,128)S(1)}, u32[]{:S(2)}, u32[]{:S(2)}) async-start(f32[32,2,128]{2,1,0:T(2,128)} %get-tuple-element.21), calls=%async_computation.14 | async-start | bytes 65536 | tf_op jit(solution)/shard_map/all_to_all | solution.py:73
  (7 other events, 145.9 us)
where the time goes:
time: 1090 us
  blocking collectives  731 us (67%)
  starting transfers between devices  159 us (15%)
  waiting for transfers between devices  132 us (12%)
  matrix products  24.9 us (2%)
  local copies, waits for them, and re-layouts  17.9 us (2%)
  other arithmetic  12.5 us (1%)
    psum x7, blocking collectives, multiply(): return lax.psum(summed, 'band')  396 us
    psum x2, blocking collectives, on_device(): current_residual_product = lax.psum(jnp.sum(residual * scaled), 'row')  121 us
    psum x2, blocking collectives, on_device(): curvature = lax.psum(jnp.sum(direction * curved), 'row')  121 us
    psum x2, blocking collectives, on_device(): rho_next = lax.psum(jnp.sum(residual * scaled), 'row')  92.8 us
    ppermute x14, starting transfers between devices, shifted(): lax.ppermute(value, axis, [(source, source + steps) for source in range(l...  87.9 us
    all_to_all x7, waiting for transfers between devices, multiply(): lax.all_to_all(far_backward, 'row', split_axis=0, concat_axis=0, tiled=True)  82.6 us
    all_to_all x7, waiting for transfers between devices, multiply(): lax.all_to_all(outgoing, 'row', split_axis=0, concat_axis=0, tiled=True)  44.9 us
    all_to_all x7, starting transfers between devices, multiply(): lax.all_to_all(far_backward, 'row', split_axis=0, concat_axis=0, tiled=True)  32.8 us
  transfers between devices with their start and end apart: 29, of which 15 were waited for; matrix products, arithmetic and copies ran while one was open for 4% of the time, Pallas kernels for 0%

commit v1 on v0

--- a/solution.py
+++ b/solution.py
@@ -80,7 +80,7 @@
         )
         carried = shifted(spread[rows_dev:], "row", 1)
         summed = jnp.concatenate([summed[:band_count] + carried, summed[band_count:]], 0)
-        return lax.psum(summed, "band")
+        return jnp.sum(lax.all_gather(summed, "band"), axis=0)
 
     row_sums = multiply(jnp.ones((rows_dev, block_size), jnp.float32))
     scaling = 1.0 / jnp.sqrt(row_sums)

time: 1090 us -> 755 us (0.69)
  blocking collectives: 731 us -> 423 us
  starting transfers between devices: 159 us -> 133 us
    psum x7 -> x0, blocking collectives: 396 us -> none  [multiply(): return lax.psum(summed, 'band')]
    all_gather x0 -> x7, blocking collectives: none -> 121 us  [multiply(): return jnp.sum(lax.all_gather(summed, 'band'), axis=0)]
    ppermute x14, starting transfers between devices: 87.9 us -> 62.4 us  [shifted(): lax.ppermute(value, axis, [(source, source + steps) for source in range(l...]
    psum x2, blocking collectives: 121 us -> 104 us  [on_device(): current_residual_product = lax.psum(jnp.sum(residual * scaled), 'row')]
    psum x2, blocking collectives: 121 us -> 104 us  [on_device(): curvature = lax.psum(jnp.sum(direction * curved), 'row')]
  transfers between devices with their start and end apart: 29 -> 29, of which waited for: 15 -> 15; matrix products, arithmetic and copies ran while one was open for 4% -> 5% of each run, Pallas kernels for 0% -> 0%
where the time goes in v1:
time: 755 us; the launch traced here: 753 us
  blocking collectives  423 us (56%)
  starting transfers between devices  133 us (18%)
  waiting for transfers between devices  132 us (17%)
  matrix products  24.9 us (3%)
  local copies, waits for them, and re-layouts  17.9 us (2%)
  other arithmetic  12.6 us (2%)
  between operations  9.3 us (1%)
    all_gather x7, blocking collectives, multiply(): return jnp.sum(lax.all_gather(summed, 'band'), axis=0)  121 us
    psum x2, blocking collectives, on_device(): curvature = lax.psum(jnp.sum(direction * curved), 'row')  104 us
    psum x2, blocking collectives, on_device(): current_residual_product = lax.psum(jnp.sum(residual * scaled), 'row')  104 us
    psum x2, blocking collectives, on_device(): rho_next = lax.psum(jnp.sum(residual * scaled), 'row')  93 us
    all_to_all x7, waiting for transfers between devices, multiply(): lax.all_to_all(far_backward, 'row', split_axis=0, concat_axis=0, tiled=True)  82.6 us
    ppermute x14, starting transfers between devices, shifted(): lax.ppermute(value, axis, [(source, source + steps) for source in range(l...  62.4 us
    all_to_all x7, waiting for transfers between devices, multiply(): lax.all_to_all(outgoing, 'row', split_axis=0, concat_axis=0, tiled=True)  44.9 us
    all_to_all x7, starting transfers between devices, multiply(): lax.all_to_all(far_backward, 'row', split_axis=0, concat_axis=0, tiled=True)  32.8 us
  transfers between devices with their start and end apart: 29, of which 15 were waited for; matrix products, arithmetic and copies ran while one was open for 5% of the time, Pallas kernels for 0%

profile of v1, /device:TPU:1, one launch (start us, length us, event | category | flops | bytes accessed | tf_op | source)
XLA Modules:
  0.0 753.2 jit_solution(9291925278446582171)
XLA Ops:
  0.7 9.0 %collective-permute-start = (bf16[16,128]{1,0:T(8,128)(2,1)S(1)}, bf16[16,128]{1,0:T(8,128)(2,1)S(1)}, u32[]{:S(2)}, u32[]{:S(2)}) collective-permute-start(bf16[16,128]{1,0:T(8,128)(2,1)S(1)} %slice.105), channel_id=1, source_target_pairs={{16,0},{32,16},{48,32},{64,48},{80,64},{96,80},{112,96},{128,112},... | collective-permute-start | bytes 12296 | tf_op jit(solution)/shard_map/ppermute | solution.py:13
  11.1 10.0 %all-to-all-start = ((s32[32,1,2]{2,1,0:T(1,128)}), s32[32,1,2]{2,1,0:T(1,128)S(1)}, u32[]{:S(2)}, u32[]{:S(2)}) async-start(s32[32,1,2]{2,1,0:T(1,128)} %copy.16), calls=%async_computation | async-start | bytes 32768 | tf_op jit(solution)/shard_map/all_to_all | solution.py:33
  59.5 12.0 %all-to-all-done.2 = f32[32,2,128]{2,1,0:T(2,128)S(1)} async-done(((f32[32,2,128]{2,1,0:T(2,128)}), f32[32,2,128]{2,1,0:T(2,128)S(1)}, u32[]{:S(2)}, u32[]{:S(2)}) %all-to-all-start.2) | async-done | bytes 32800 | tf_op jit(solution)/shard_map/all_to_all | solution.py:73
  71.8 18.8 %all-gather = f32[512,128]{1,0:T(8,128)S(1)} all-gather(f32[32,128]{1,0:T(8,128)S(1)} %pad_maximum_fusion), channel_id=2, replica_groups=mesh['row'=32,'band'=16] {'band'}, dimensions={0}, use_global_device_ids=true | all-gather | bytes 278528 | tf_op jit(solution)/shard_map/all_gather | solution.py:83
  122.3 11.8 %all-to-all-done.4 = f32[32,2,128]{2,1,0:T(2,128)S(1)} async-done(((f32[32,2,128]{2,1,0:T(2,128)}), f32[32,2,128]{2,1,0:T(2,128)S(1)}, u32[]{:S(2)}, u32[]{:S(2)}) %all-to-all-start.4) | async-done | bytes 32800 | tf_op jit(solution)/shard_map/all_to_all | solution.py:73
  134.4 17.9 %all-gather.1 = f32[512,128]{1,0:T(8,128)S(1)} all-gather(f32[32,128]{1,0:T(8,128)S(1)} %pad_maximum_fusion.1), channel_id=3, replica_groups=mesh['row'=32,'band'=16] {'band'}, dimensions={0}, use_global_device_ids=true | all-gather | bytes 278528 | tf_op jit(solution)/shard_map/all_gather | solution.py:83
  154.2 8.2 %collective-permute-start.4 = (bf16[16,128]{1,0:T(8,128)(2,1)S(1)}, bf16[16,128]{1,0:T(8,128)(2,1)S(1)}, u32[]{:S(2)}, u32[]{:S(2)}) collective-permute-start(bf16[16,128]{1,0:T(8,128)(2,1)S(1)} %slice.177), channel_id=1, source_target_pairs={{16,0},{32,16},{48,32},{64,48},{80,64},{96,80},{112,96},{128,112},... | collective-permute-start | bytes 12296 | tf_op jit(solution)/shard_map/ppermute | solution.py:13
  184.1 11.8 %all-to-all-done.6 = f32[32,2,128]{2,1,0:T(2,128)S(1)} async-done(((f32[32,2,128]{2,1,0:T(2,128)}), f32[32,2,128]{2,1,0:T(2,128)S(1)}, u32[]{:S(2)}, u32[]{:S(2)}) %all-to-all-start.6) | async-done | bytes 32800 | tf_op jit(solution)/shard_map/all_to_all | solution.py:73
  196.2 16.2 %all-gather.2 = f32[512,128]{1,0:T(8,128)S(1)} all-gather(f32[32,128]{1,0:T(8,128)S(1)} %pad_maximum_fusion.2), channel_id=4, replica_groups=mesh['row'=32,'band'=16] {'band'}, dimensions={0}, use_global_device_ids=true | all-gather | bytes 278528 | tf_op jit(solution)/shard_map/all_gather | solution.py:83
  213.1 52.2 %all-reduce.2 = (f32[]{:T(128)}, f32[]{:T(128)}) all-reduce(f32[]{:T(128)} %get-tuple-element.3, f32[]{:T(128)} %get-tuple-element.2), channel_id=1, replica_groups=mesh['row'=32,'band'=16] {'row'}, use_global_device_ids=true, to_apply=%region_3.0 | all-reduce | flops 2 | bytes 16 | tf_op jit(solution)/shard_map/psum | solution.py:93
  267.3 46.6 %psum.58 = f32[]{:T(128)} all-reduce(f32[]{:T(128)} %multiply_reduce_fusion.4), channel_id=1, replica_groups=mesh['row'=32,'band'=16] {'row'}, use_global_device_ids=true, to_apply=%region_8.0 | all-reduce | flops 1 | bytes 8 | tf_op jit(solution)/shard_map/psum | solution.py:103
  341.2 11.8 %all-to-all-done.8 = f32[32,2,128]{2,1,0:T(2,128)S(1)} async-done(((f32[32,2,128]{2,1,0:T(2,128)}), f32[32,2,128]{2,1,0:T(2,128)S(1)}, u32[]{:S(2)}, u32[]{:S(2)}) %all-to-all-start.8) | async-done | bytes 32800 | tf_op jit(solution)/shard_map/all_to_all | solution.py:73
  353.3 17.9 %all-gather.3 = f32[512,128]{1,0:T(8,128)S(1)} all-gather(f32[32,128]{1,0:T(8,128)S(1)} %pad_maximum_fusion.3), channel_id=5, replica_groups=mesh['row'=32,'band'=16] {'band'}, dimensions={0}, use_global_device_ids=true | all-gather | bytes 278528 | tf_op jit(solution)/shard_map/all_gather | solution.py:83
  371.8 52.1 %psum.59 = f32[]{:T(128)} all-reduce(f32[]{:T(128)} %multiply_reduce_fusion.3), channel_id=1, replica_groups=mesh['row'=32,'band'=16] {'row'}, use_global_device_ids=true, to_apply=%region_11.0 | all-reduce | flops 1 | bytes 8 | tf_op jit(solution)/shard_map/psum | solution.py:97
  451.2 11.8 %all-to-all-done.10 = f32[32,2,128]{2,1,0:T(2,128)S(1)} async-done(((f32[32,2,128]{2,1,0:T(2,128)}), f32[32,2,128]{2,1,0:T(2,128)S(1)}, u32[]{:S(2)}, u32[]{:S(2)}) %all-to-all-start.10) | async-done | bytes 32800 | tf_op jit(solution)/shard_map/all_to_all | solution.py:73
  463.3 16.2 %all-gather.4 = f32[512,128]{1,0:T(8,128)S(1)} all-gather(f32[32,128]{1,0:T(8,128)S(1)} %pad_maximum_fusion.4), channel_id=6, replica_groups=mesh['row'=32,'band'=16] {'band'}, dimensions={0}, use_global_device_ids=true | all-gather | bytes 278528 | tf_op jit(solution)/shard_map/all_gather | solution.py:83
  481.5 8.4 %collective-permute-start.10 = (bf16[16,128]{1,0:T(8,128)(2,1)S(1)}, bf16[16,128]{1,0:T(8,128)(2,1)S(1)}, u32[]{:S(2)}, u32[]{:S(2)}) collective-permute-start(bf16[16,128]{1,0:T(8,128)(2,1)S(1)} %slice.192), channel_id=1, source_target_pairs={{16,0},{32,16},{48,32},{64,48},{80,64},{96,80},{112,96},{128,112},... | collective-permute-start | bytes 12296 | tf_op jit(solution)/shard_map/ppermute | solution.py:13
  511.5 11.8 %all-to-all-done.12 = f32[32,2,128]{2,1,0:T(2,128)S(1)} async-done(((f32[32,2,128]{2,1,0:T(2,128)}), f32[32,2,128]{2,1,0:T(2,128)S(1)}, u32[]{:S(2)}, u32[]{:S(2)}) %all-to-all-start.12) | async-done | bytes 32800 | tf_op jit(solution)/shard_map/all_to_all | solution.py:73
  523.6 17.9 %all-gather.5 = f32[512,128]{1,0:T(8,128)S(1)} all-gather(f32[32,128]{1,0:T(8,128)S(1)} %pad_maximum_fusion.5), channel_id=7, replica_groups=mesh['row'=32,'band'=16] {'band'}, dimensions={0}, use_global_device_ids=true | all-gather | bytes 278528 | tf_op jit(solution)/shard_map/all_gather | solution.py:83
  542.1 52.1 %all-reduce.1 = (f32[]{:T(128)}, f32[]{:T(128)}) all-reduce(f32[]{:T(128)} %get-tuple-element.5, f32[]{:T(128)} %get-tuple-element.4), channel_id=1, replica_groups=mesh['row'=32,'band'=16] {'row'}, use_global_device_ids=true, to_apply=%region_14.0 | all-reduce | flops 2 | bytes 16 | tf_op jit(solution)/shard_map/psum | solution.py:93
  596.2 46.4 %psum.62 = f32[]{:T(128)} all-reduce(f32[]{:T(128)} %get-tuple-element.10), channel_id=1, replica_groups=mesh['row'=32,'band'=16] {'row'}, use_global_device_ids=true, to_apply=%region_19.0 | all-reduce | flops 1 | bytes 8 | tf_op jit(solution)/shard_map/psum | solution.py:103
  670.1 11.8 %all-to-all-done.14 = f32[32,2,128]{2,1,0:T(2,128)S(1)} async-done(((f32[32,2,128]{2,1,0:T(2,128)}), f32[32,2,128]{2,1,0:T(2,128)S(1)}, u32[]{:S(2)}, u32[]{:S(2)}) %all-to-all-start.14) | async-done | bytes 32800 | tf_op jit(solution)/shard_map/all_to_all | solution.py:73
  682.2 16.2 %all-gather.6 = f32[512,128]{1,0:T(8,128)S(1)} all-gather(f32[32,128]{1,0:T(8,128)S(1)} %pad_maximum_fusion.6), channel_id=8, replica_groups=mesh['row'=32,'band'=16] {'band'}, dimensions={0}, use_global_device_ids=true | all-gather | bytes 278528 | tf_op jit(solution)/shard_map/all_gather | solution.py:83
  699.0 52.3 %psum.63 = f32[]{:T(128)} all-reduce(f32[]{:T(128)} %multiply_reduce_fusion), channel_id=1, replica_groups=mesh['row'=32,'band'=16] {'row'}, use_global_device_ids=true, to_apply=%region_22.0 | all-reduce | flops 1 | bytes 8 | tf_op jit(solution)/shard_map/psum | solution.py:97
  (209 shorter events, 202.8 us)
Async XLA Ops:
  0.7 43.3 %collective-permute-start = (bf16[16,128]{1,0:T(8,128)(2,1)S(1)}, bf16[16,128]{1,0:T(8,128)(2,1)S(1)}, u32[]{:S(2)}, u32[]{:S(2)}) collective-permute-start(bf16[16,128]{1,0:T(8,128)(2,1)S(1)} %slice.105), channel_id=1, source_target_pairs={{16,0},{32,16},{48,32},{64,48},{80,64},{96,80},{112,96},{128,112},... | collective-permute-start | bytes 12296 | tf_op jit(solution)/shard_map/ppermute | solution.py:13
  11.1 21.8 %all-to-all-start = ((s32[32,1,2]{2,1,0:T(1,128)}), s32[32,1,2]{2,1,0:T(1,128)S(1)}, u32[]{:S(2)}, u32[]{:S(2)}) async-start(s32[32,1,2]{2,1,0:T(1,128)} %copy.16), calls=%async_computation | async-start | bytes 32768 | tf_op jit(solution)/shard_map/all_to_all | solution.py:33
  23.0 48.8 %collective-permute-start.1 = (f32[16,128]{1,0:T(8,128)S(1)}, f32[16,128]{1,0:T(8,128)S(1)}, u32[]{:S(2)}, u32[]{:S(2)}) collective-permute-start(f32[16,128]{1,0:T(8,128)S(1)} %slice.170), channel_id=1, source_target_pairs={{0,16},{16,32},{32,48},{48,64},{64,80},{80,96},{96,112},{112,128},... | collective-permute-start | bytes 24584 | tf_op jit(solution)/shard_map/ppermute | solution.py:13
  35.0 17.9 %all-to-all-start.1 = ((bf16[32,2,128]{2,1,0:T(2,128)(2,1)}), bf16[32,2,128]{2,1,0:T(2,128)(2,1)S(1)}, u32[]{:S(2)}, u32[]{:S(2)}) async-start(bf16[32,2,128]{2,1,0:T(2,128)(2,1)} %bitcast.8), calls=%async_computation.1 | async-start | bytes 32768 | tf_op jit(solution)/shard_map/all_to_all | solution.py:54
  54.8 16.6 %all-to-all-start.2 = ((f32[32,2,128]{2,1,0:T(2,128)}), f32[32,2,128]{2,1,0:T(2,128)S(1)}, u32[]{:S(2)}, u32[]{:S(2)}) async-start(f32[32,2,128]{2,1,0:T(2,128)} %get-tuple-element.45), calls=%async_computation.2 | async-start | bytes 65536 | tf_op jit(solution)/shard_map/all_to_all | solution.py:73
  92.5 16.0 %collective-permute-start.2 = (bf16[16,128]{1,0:T(8,128)(2,1)S(1)}, bf16[16,128]{1,0:T(8,128)(2,1)S(1)}, u32[]{:S(2)}, u32[]{:S(2)}) collective-permute-start(bf16[16,128]{1,0:T(8,128)(2,1)S(1)} %slice.172), channel_id=1, source_target_pairs={{16,0},{32,16},{48,32},{64,48},{80,64},{96,80},{112,96},{128,112},... | collective-permute-start | bytes 12296 | tf_op jit(solution)/shard_map/ppermute | solution.py:13
  100.7 14.7 %all-to-all-start.3 = ((bf16[32,2,128]{2,1,0:T(2,128)(2,1)}), bf16[32,2,128]{2,1,0:T(2,128)(2,1)S(1)}, u32[]{:S(2)}, u32[]{:S(2)}) async-start(bf16[32,2,128]{2,1,0:T(2,128)(2,1)} %bitcast.28), calls=%async_computation.3 | async-start | bytes 32768 | tf_op jit(solution)/shard_map/all_to_all | solution.py:54
  105.7 28.7 %collective-permute-start.3 = (f32[16,128]{1,0:T(8,128)S(1)}, f32[16,128]{1,0:T(8,128)S(1)}, u32[]{:S(2)}, u32[]{:S(2)}) collective-permute-start(f32[16,128]{1,0:T(8,128)S(1)} %slice.175), channel_id=1, source_target_pairs={{0,16},{16,32},{32,48},{48,64},{64,80},{80,96},{96,112},{112,128},... | collective-permute-start | bytes 24584 | tf_op jit(solution)/shard_map/ppermute | solution.py:13
  117.3 16.8 %all-to-all-start.4 = ((f32[32,2,128]{2,1,0:T(2,128)}), f32[32,2,128]{2,1,0:T(2,128)S(1)}, u32[]{:S(2)}, u32[]{:S(2)}) async-start(f32[32,2,128]{2,1,0:T(2,128)} %get-tuple-element.41), calls=%async_computation.4 | async-start | bytes 65536 | tf_op jit(solution)/shard_map/all_to_all | solution.py:73
  154.2 16.0 %collective-permute-start.4 = (bf16[16,128]{1,0:T(8,128)(2,1)S(1)}, bf16[16,128]{1,0:T(8,128)(2,1)S(1)}, u32[]{:S(2)}, u32[]{:S(2)}) collective-permute-start(bf16[16,128]{1,0:T(8,128)(2,1)S(1)} %slice.177), channel_id=1, source_target_pairs={{16,0},{32,16},{48,32},{64,48},{80,64},{96,80},{112,96},{128,112},... | collective-permute-start | bytes 12296 | tf_op jit(solution)/shard_map/ppermute | solution.py:13
  162.5 14.7 %all-to-all-start.5 = ((bf16[32,2,128]{2,1,0:T(2,128)(2,1)}), bf16[32,2,128]{2,1,0:T(2,128)(2,1)S(1)}, u32[]{:S(2)}, u32[]{:S(2)}) async-start(bf16[32,2,128]{2,1,0:T(2,128)(2,1)} %bitcast.45), calls=%async_computation.5 | async-start | bytes 32768 | tf_op jit(solution)/shard_map/all_to_all | solution.py:54
  167.5 28.7 %collective-permute-start.5 = (f32[16,128]{1,0:T(8,128)S(1)}, f32[16,128]{1,0:T(8,128)S(1)}, u32[]{:S(2)}, u32[]{:S(2)}) collective-permute-start(f32[16,128]{1,0:T(8,128)S(1)} %slice.180), channel_id=1, source_target_pairs={{0,16},{16,32},{32,48},{48,64},{64,80},{80,96},{96,112},{112,128},... | collective-permute-start | bytes 24584 | tf_op jit(solution)/shard_map/ppermute | solution.py:13
  179.1 16.8 %all-to-all-start.6 = ((f32[32,2,128]{2,1,0:T(2,128)}), f32[32,2,128]{2,1,0:T(2,128)S(1)}, u32[]{:S(2)}, u32[]{:S(2)}) async-start(f32[32,2,128]{2,1,0:T(2,128)} %get-tuple-element.37), calls=%async_computation.6 | async-start | bytes 65536 | tf_op jit(solution)/shard_map/all_to_all | solution.py:73
  324.5 28.7 %collective-permute-start.7 = (f32[16,128]{1,0:T(8,128)S(1)}, f32[16,128]{1,0:T(8,128)S(1)}, u32[]{:S(2)}, u32[]{:S(2)}) collective-permute-start(f32[16,128]{1,0:T(8,128)S(1)} %slice.185), channel_id=1, source_target_pairs={{0,16},{16,32},{32,48},{48,64},{64,80},{80,96},{96,112},{112,128},... | collective-permute-start | bytes 24584 | tf_op jit(solution)/shard_map/ppermute | solution.py:13
  336.1 16.8 %all-to-all-start.8 = ((f32[32,2,128]{2,1,0:T(2,128)}), f32[32,2,128]{2,1,0:T(2,128)S(1)}, u32[]{:S(2)}, u32[]{:S(2)}) async-start(f32[32,2,128]{2,1,0:T(2,128)} %get-tuple-element.33), calls=%async_computation.8 | async-start | bytes 65536 | tf_op jit(solution)/shard_map/all_to_all | solution.py:73
  434.6 28.7 %collective-permute-start.9 = (f32[16,128]{1,0:T(8,128)S(1)}, f32[16,128]{1,0:T(8,128)S(1)}, u32[]{:S(2)}, u32[]{:S(2)}) collective-permute-start(f32[16,128]{1,0:T(8,128)S(1)} %slice.190), channel_id=1, source_target_pairs={{0,16},{16,32},{32,48},{48,64},{64,80},{80,96},{96,112},{112,128},... | collective-permute-start | bytes 24584 | tf_op jit(solution)/shard_map/ppermute | solution.py:13
  446.2 16.8 %all-to-all-start.10 = ((f32[32,2,128]{2,1,0:T(2,128)}), f32[32,2,128]{2,1,0:T(2,128)S(1)}, u32[]{:S(2)}, u32[]{:S(2)}) async-start(f32[32,2,128]{2,1,0:T(2,128)} %get-tuple-element.29), calls=%async_computation.10 | async-start | bytes 65536 | tf_op jit(solution)/shard_map/all_to_all | solution.py:73
  481.5 16.1 %collective-permute-start.10 = (bf16[16,128]{1,0:T(8,128)(2,1)S(1)}, bf16[16,128]{1,0:T(8,128)(2,1)S(1)}, u32[]{:S(2)}, u32[]{:S(2)}) collective-permute-start(bf16[16,128]{1,0:T(8,128)(2,1)S(1)} %slice.192), channel_id=1, source_target_pairs={{16,0},{32,16},{48,32},{64,48},{80,64},{96,80},{112,96},{128,112},... | collective-permute-start | bytes 12296 | tf_op jit(solution)/shard_map/ppermute | solution.py:13
  489.9 14.7 %all-to-all-start.11 = ((bf16[32,2,128]{2,1,0:T(2,128)(2,1)}), bf16[32,2,128]{2,1,0:T(2,128)(2,1)S(1)}, u32[]{:S(2)}, u32[]{:S(2)}) async-start(bf16[32,2,128]{2,1,0:T(2,128)(2,1)} %bitcast.96), calls=%async_computation.11 | async-start | bytes 32768 | tf_op jit(solution)/shard_map/all_to_all | solution.py:54
  494.8 28.7 %collective-permute-start.11 = (f32[16,128]{1,0:T(8,128)S(1)}, f32[16,128]{1,0:T(8,128)S(1)}, u32[]{:S(2)}, u32[]{:S(2)}) collective-permute-start(f32[16,128]{1,0:T(8,128)S(1)} %slice.195), channel_id=1, source_target_pairs={{0,16},{16,32},{32,48},{48,64},{64,80},{80,96},{96,112},{112,128},... | collective-permute-start | bytes 24584 | tf_op jit(solution)/shard_map/ppermute | solution.py:13
  506.5 16.8 %all-to-all-start.12 = ((f32[32,2,128]{2,1,0:T(2,128)}), f32[32,2,128]{2,1,0:T(2,128)S(1)}, u32[]{:S(2)}, u32[]{:S(2)}) async-start(f32[32,2,128]{2,1,0:T(2,128)} %get-tuple-element.25), calls=%async_computation.12 | async-start | bytes 65536 | tf_op jit(solution)/shard_map/all_to_all | solution.py:73
  648.3 14.9 %all-to-all-start.13 = ((bf16[32,2,128]{2,1,0:T(2,128)(2,1)}), bf16[32,2,128]{2,1,0:T(2,128)(2,1)S(1)}, u32[]{:S(2)}, u32[]{:S(2)}) async-start(bf16[32,2,128]{2,1,0:T(2,128)(2,1)} %bitcast.113), calls=%async_computation.13 | async-start | bytes 32768 | tf_op jit(solution)/shard_map/all_to_all | solution.py:54
  653.5 28.7 %collective-permute-start.13 = (f32[16,128]{1,0:T(8,128)S(1)}, f32[16,128]{1,0:T(8,128)S(1)}, u32[]{:S(2)}, u32[]{:S(2)}) collective-permute-start(f32[16,128]{1,0:T(8,128)S(1)} %slice.200), channel_id=1, source_target_pairs={{0,16},{16,32},{32,48},{48,64},{64,80},{80,96},{96,112},{112,128},... | collective-permute-start | bytes 24584 | tf_op jit(solution)/shard_map/ppermute | solution.py:13
  665.1 16.8 %all-to-all-start.14 = ((f32[32,2,128]{2,1,0:T(2,128)}), f32[32,2,128]{2,1,0:T(2,128)S(1)}, u32[]{:S(2)}, u32[]{:S(2)}) async-start(f32[32,2,128]{2,1,0:T(2,128)} %get-tuple-element.21), calls=%async_computation.14 | async-start | bytes 65536 | tf_op jit(solution)/shard_map/all_to_all | solution.py:73
  (7 other events, 146.0 us)
